TPU v7x, 256 devices: a whole 4x4x8 slice. The times are simulated.
256 devices in a mesh: row: 16 (over z, core), col: 16 (over y, x).
Axes of the slice: x: 4, y: 4, z: 8, core: 2. Of those that a mesh axis runs over, the one named last changes fastest.
Arguments:
- prior_window_motion: float32 [3, 128, 128, 256], P(None, 'row', 'col'), may hold values from -1.2 to 1.2
- prior_window_stress: float32 [128, 128, 256], P('row', 'col'), may hold values from -3 to 3
- heat_scalar: float32 [128, 128, 256], P('row', 'col'), may hold values from 0 to 1
Outputs:
- velocity: float32 [3, 128, 128, 256], P(None, 'row', 'col')
- pressure: float32 [128, 128, 256], P('row', 'col')
All inputs are finite; a program needn't handle non-finite values.
Results may differ from a plain program's by a relative error of at most 0.0003.
Values sent between devices are 32-bit elements; how exact they have to be, the bound alone decides.
No kernel may reach another device: no remote copies, remote signals or barrier semaphores. Data moves between devices by JAX's collectives and lax.ppermute only.
A program may use at most 64 MiB of HBM per device.

v0:
```python
import jax
import jax.numpy as jnp
from jax import lax
from jax.sharding import PartitionSpec as P

OUTER = 2
INNER = 2
PRECISE = lax.Precision.HIGHEST
ENABLE_SWITCH = 2.0
OFFSET_COUNT = 0.5
AUGMENT = 1.0
ANCHOR = 0.002
RAYLEIGH_NUMBER = 1.0
SMOOTHING = 2.0


def padded(cells, sides, width):
    for axis, dim in sides:
        count = lax.axis_size(axis)
        head = lax.slice_in_dim(cells, 0, width, axis=dim)
        tail = lax.slice_in_dim(cells, cells.shape[dim] - width, cells.shape[dim], axis=dim)
        cells = jnp.concatenate(
            [
                lax.ppermute(tail, axis, [(i, (i + 1) % count) for i in range(count)]),
                cells,
                lax.ppermute(head, axis, [((i + 1) % count, i) for i in range(count)]),
            ],
            axis=dim,
        )
    return cells


def global_sum(value):
    count = lax.axis_size("row") * lax.axis_size("col")
    spread = jnp.broadcast_to(value.reshape(1), (count,))
    gathered = lax.all_to_all(spread, ("row", "col"), 0, 0, tiled=True)
    return jnp.sum(gathered)


def from_behind(value, axis, steps):
    count = lax.axis_size(axis)
    pairs = [(source, (source + steps) % count) for source in range(count)]
    return lax.ppermute(value, axis, pairs)


def cas_matrix(extent):
    index = jnp.arange(extent, dtype=jnp.int32)
    phase = index[:, None] * index[None, :] % extent
    angle = 2.0 * jnp.pi / extent * phase.astype(jnp.float32)
    return jnp.cos(angle) + jnp.sin(angle)


def eigen_row(number, offset_index, extent):
    index = offset_index + jnp.arange(number, dtype=jnp.int32)
    return 2.0 - 2.0 * jnp.cos(2.0 * jnp.pi / extent * index.astype(jnp.float32))


def precondition(residual, tables):
    xtable, ytable, ztable = tables
    row_count = lax.axis_size("row")
    col_count = lax.axis_size("col")
    components, owned_height_lines, owned_depth_slices, period_extent_first = residual.shape
    ylength = owned_height_lines * row_count
    zlength = owned_depth_slices * col_count
    normal_factor = 1.0 / (period_extent_first * ylength * zlength)
    xpiece = period_extent_first // row_count
    ypiece = ylength // col_count
    spectrum = jnp.einsum("kx,cyzx->cykz", xtable, residual, precision=PRECISE).reshape(
        components, owned_height_lines, period_extent_first * owned_depth_slices
    )
    spectrum = lax.all_to_all(spectrum, "row", split_axis=2, concat_axis=1, tiled=True)
    spectrum = jnp.einsum(
        "ky,cyxz->czkx",
        ytable,
        spectrum.reshape(components, ylength, xpiece, owned_depth_slices),
        precision=PRECISE,
    ).reshape(components, owned_depth_slices, ylength * xpiece)
    spectrum = lax.all_to_all(spectrum, "col", split_axis=2, concat_axis=1, tiled=True)
    zeigen = eigen_row(zlength, 0, zlength)
    yeigen = eigen_row(ypiece, lax.axis_index("col") * ypiece, ylength)
    xeigen = eigen_row(xpiece, lax.axis_index("row") * xpiece, period_extent_first)
    mixed_eigen = (yeigen[:, None] + xeigen[None, :]).reshape(-1)
    symbol = normal_factor / (SMOOTHING * (zeigen[:, None] + mixed_eigen[None, :]) + ANCHOR)
    spectrum = jnp.einsum("kz,czm->ckm", ztable, spectrum, precision=PRECISE)
    spectrum = jnp.einsum("kz,czm->ckm", ztable, spectrum * symbol[None], precision=PRECISE)
    spectrum = lax.all_to_all(spectrum, "col", split_axis=1, concat_axis=2, tiled=True)
    spectrum = jnp.einsum(
        "ky,czyx->ckxz",
        ytable,
        spectrum.reshape(components, owned_depth_slices, ylength, xpiece),
        precision=PRECISE,
    ).reshape(components, ylength, xpiece * owned_depth_slices)
    spectrum = lax.all_to_all(spectrum, "row", split_axis=1, concat_axis=2, tiled=True)
    return jnp.einsum(
        "kx,cyxz->cyzk",
        xtable,
        spectrum.reshape(components, owned_height_lines, period_extent_first, owned_depth_slices),
        precision=PRECISE,
    )


def forward(extended, direction):
    owned_height_lines = extended.shape[-3] - 2
    owned_depth_slices = extended.shape[-2] - 2
    root = extended[..., : owned_height_lines + 1, : owned_depth_slices + 1, :]
    if direction == 0:
        return jnp.roll(root, -1, -1) - root
    if direction == 1:
        return extended[..., 1 : owned_height_lines + 2, : owned_depth_slices + 1, :] - root
    return extended[..., : owned_height_lines + 1, 1 : owned_depth_slices + 2, :] - root


def backward(region, direction):
    center = region[..., 1:, 1:, :]
    if direction == 0:
        return center - jnp.roll(center, 1, -1)
    if direction == 1:
        return center - region[..., :-1, 1:, :]
    return center - region[..., 1:, :-1, :]


def extend(field):
    return padded(field, (("row", 1), ("col", 2)), 1)


def lower_region(pressure):
    below_y = from_behind(pressure[-1:], "row", 1)
    below_z = from_behind(pressure[:, -1:], "col", 1)
    corner = jnp.zeros((1, 1, pressure.shape[2]), jnp.float32)
    upper_band = jnp.concatenate([corner, below_y], 1)
    main_band = jnp.concatenate([below_z, pressure], 1)
    return jnp.concatenate([upper_band, main_band], 0)


def operate(extended, shear_resistance_map):
    owned_height_lines = extended.shape[1] - 2
    owned_depth_slices = extended.shape[2] - 2
    gradients = [[forward(extended[target], source) for source in range(3)] for target in range(3)]
    spread = gradients[0][0] + gradients[1][1] + gradients[2][2]
    result = []
    for target in range(3):
        summed = (
            ANCHOR * extended[target, 1 : owned_height_lines + 1, 1 : owned_depth_slices + 1, :]
        )
        for source in range(3):
            fluxes = shear_resistance_map * (gradients[target][source] + gradients[source][target])
            if target == source:
                fluxes = fluxes + AUGMENT * spread
            summed = summed - backward(fluxes, source)
        result.append(summed)
    return jnp.stack(result)


def pressure_gradient(region):
    return jnp.stack([-backward(region, target) for target in range(3)])


def divergence_region(extended):
    return forward(extended[0], 0) + forward(extended[1], 1) + forward(extended[2], 2)


def per_device(prior_window_motion, prior_window_stress, heat_scalar):
    owned_height_lines, owned_depth_slices, period_extent_first = heat_scalar.shape
    tables = (
        cas_matrix(period_extent_first),
        cas_matrix(owned_height_lines * lax.axis_size("row")),
        cas_matrix(owned_depth_slices * lax.axis_size("col")),
    )
    stacked_fields = jnp.concatenate(
        [prior_window_motion, prior_window_stress[None], heat_scalar[None]], 0
    )
    extended = padded(stacked_fields, (("row", 1), ("col", 2)), 1)
    shear_resistance_map = jnp.exp(
        ENABLE_SWITCH
        * (
            1.0
            / (extended[4, : owned_height_lines + 1, : owned_depth_slices + 1, :] + OFFSET_COUNT)
            - 1.0 / (0.5 + OFFSET_COUNT)
        )
    )
    thermal_lift = RAYLEIGH_NUMBER * (heat_scalar - 0.5)
    zeroes = jnp.zeros_like(thermal_lift)
    forcing = jnp.stack([zeroes, zeroes, thermal_lift])
    velocity = prior_window_motion
    pressure = prior_window_stress
    velocity_ext = extended[0:3]
    pushing = pressure_gradient(extended[3, : owned_height_lines + 1, : owned_depth_slices + 1, :])
    spread_now = jnp.zeros_like(shear_resistance_map)
    for outer_step in range(OUTER):
        if outer_step > 0:
            pushing = pressure_gradient(lower_region(pressure))
        residual = forcing - pushing - operate(velocity_ext, shear_resistance_map)
        direction = residual
        image = residual
        energy_now = jnp.float32(1.0)
        step_size = jnp.float32(1.0)
        for inner_step in range(INNER):
            precond = precondition(residual, tables)
            energy_next = global_sum(jnp.sum(residual * precond))
            if inner_step == 0:
                direction = precond
            else:
                direction = precond + energy_next / energy_now * direction
            energy_now = energy_next
            image = operate(extend(direction), shear_resistance_map)
            curvature = global_sum(jnp.sum(direction * image))
            step_size = energy_now / curvature
            velocity = velocity + step_size * direction
            residual = residual - step_size * image
        velocity_ext = extend(velocity)
        spread_now = divergence_region(velocity_ext)
        pressure = pressure + AUGMENT * spread_now[1:, 1:, :]
    return (velocity, pressure)


def solution(mesh):
    placed = (P(None, "row", "col", None), P("row", "col", None), P("row", "col", None))
    return jax.shard_map(
        per_device,
        mesh=mesh,
        in_specs=placed,
        out_specs=(P(None, "row", "col", None), P("row", "col", None)),
        check_vma=False,
    )
```

profile of v0, /device:TPU:30, one launch (start us, length us, event | category | flops | bytes accessed | tf_op | source)
XLA Modules:
  0.0 742.4 jit_solution(7646809558216230969)
XLA Ops:
  31.7 6.4 all-to-all-start
  39.5 8.6 %all-to-all-done = f32[16,1,3072]{2,1,0:T(1,128)S(1)} async-done(((f32[16,1,3072]{2,1,0:T(1,128)}), f32[16,1,3072]{2,1,0:T(1,128)S(1)}, u32[]{:S(2)}, u32[]{:S(2)}) %all-to-all-start) | async-done | bytes 196640 | tf_op jit(solution)/shard_map/all_to_all | solution.py:71
  60.6 5.9 fusion.8
  76.0 6.7 all-to-all-start.1
  97.4 12.2 %all_to_all.300 = f32[3,128,128]{2,0,1:T(4,128)S(1)} all-to-all(f32[3,128,128]{2,0,1:T(4,128)S(1)} %copy.371), channel_id=1, replica_groups=mesh['row'=16,'col'=16] {'col'}, dimensions={1} | all-to-all | bytes 393216 | tf_op jit(solution)/shard_map/all_to_all | solution.py:86
  112.9 13.7 %all_to_all.301 = f32[3,128,128]{2,0,1:T(4,128)S(1)} all-to-all(f32[3,128,128]{2,0,1:T(4,128)S(1)} %copy.376), channel_id=1, replica_groups=mesh['row'=16,'col'=16] {'row'}, dimensions={1} | all-to-all | bytes 393216 | tf_op jit(solution)/shard_map/all_to_all | solution.py:93
  154.3 18.4 %all_to_all.302 = f32[256,1,1]{2,1,0:T(1,128)S(1)} all-to-all(f32[256,1,1]{2,1,0:T(1,128)S(1)} %broadcast_in_dim.23), channel_id=1, replica_groups=mesh['row'=16,'col'=16] {'row','col'}, dimensions={0} | all-to-all | bytes 2048 | tf_op jit(solution)/shard_map/all_to_all | solution.py:36
  174.1 9.1 %all-to-all-start.4 = ((f32[256,1,1]{2,1,0:T(1,128)}), f32[256,1,1]{2,1,0:T(1,128)S(1)}, u32[]{:S(2)}, u32[]{:S(2)}) async-start(f32[256,1,1]{2,1,0:T(1,128)} %broadcast_in_dim.22), calls=%async_computation.4 | async-start | bytes 262144 | tf_op jit(solution)/shard_map/all_to_all | solution.py:36
  184.2 8.8 %all-to-all-done.4 = f32[256,1,1]{2,1,0:T(1,128)S(1)} async-done(((f32[256,1,1]{2,1,0:T(1,128)}), f32[256,1,1]{2,1,0:T(1,128)S(1)}, u32[]{:S(2)}, u32[]{:S(2)}) %all-to-all-start.4) | async-done | bytes 1056 | tf_op jit(solution)/shard_map/all_to_all | solution.py:36
  205.6 12.5 %all_to_all.303 = f32[16,1,3072]{2,1,0:T(1,128)S(1)} all-to-all(f32[16,1,3072]{2,1,0:T(1,128)S(1)} %reshape.266), channel_id=1, replica_groups=mesh['row'=16,'col'=16] {'row'}, dimensions={0} | all-to-all | bytes 393216 | tf_op jit(solution)/shard_map/all_to_all | solution.py:71
  230.1 5.9 fusion.11
  245.0 11.3 %all_to_all.304 = f32[16,1,3072]{2,1,0:T(1,128)S(1)} all-to-all(f32[16,1,3072]{2,1,0:T(1,128)S(1)} %reshape.268), channel_id=1, replica_groups=mesh['row'=16,'col'=16] {'col'}, dimensions={0} | all-to-all | bytes 393216 | tf_op jit(solution)/shard_map/all_to_all | solution.py:78
  266.2 12.1 %all_to_all.305 = f32[3,128,128]{2,0,1:T(4,128)S(1)} all-to-all(f32[3,128,128]{2,0,1:T(4,128)S(1)} %copy.392), channel_id=1, replica_groups=mesh['row'=16,'col'=16] {'col'}, dimensions={1} | all-to-all | bytes 393216 | tf_op jit(solution)/shard_map/all_to_all | solution.py:86
  281.6 13.6 %all_to_all.306 = f32[3,128,128]{2,0,1:T(4,128)S(1)} all-to-all(f32[3,128,128]{2,0,1:T(4,128)S(1)} %copy.397), channel_id=1, replica_groups=mesh['row'=16,'col'=16] {'row'}, dimensions={1} | all-to-all | bytes 393216 | tf_op jit(solution)/shard_map/all_to_all | solution.py:93
  298.6 8.0 %multiply_reduce_fusion.3 = (f32[]{:T(128)}, f32[3,8,8,256]{3,2,1,0:T(8,128)}) fusion(f32[3,8,8,256]{3,2,1,0:T(8,128)} %copy-done.17, f32[1,8,8,256]{3,2,1,0:T(8,128)} %copy-done.23, f32[1,8,8,256]{3,2,1,0:T(8,128)} %copy-done.27, f32[1,8,8,256]{3,2,1,0:T(8,128)} %copy-done.26, f32[]{:T(128)S(6)} %div.34, f32[3,8,256,8]{3,2,1,0:T(8,128)S(1)} %reshape.245), kind=kOutput, calls=%fused_computation.94 | convolution fusion | flops 152272896 | bytes 786440 | tf_op jit(solution)/shard_map/kx,cyxz->cyzk/dot_general | solution.py:94
  307.4 18.9 %all_to_all.307 = f32[256,1,1]{2,1,0:T(1,128)S(1)} all-to-all(f32[256,1,1]{2,1,0:T(1,128)S(1)} %broadcast_in_dim.24), channel_id=1, replica_groups=mesh['row'=16,'col'=16] {'row','col'}, dimensions={0} | all-to-all | bytes 2048 | tf_op jit(solution)/shard_map/all_to_all | solution.py:36
  347.7 17.9 %all_to_all.308 = f32[256,1,1]{2,1,0:T(1,128)S(1)} all-to-all(f32[256,1,1]{2,1,0:T(1,128)S(1)} %broadcast_in_dim.25), channel_id=1, replica_groups=mesh['row'=16,'col'=16] {'row','col'}, dimensions={0} | all-to-all | bytes 2048 | tf_op jit(solution)/shard_map/all_to_all | solution.py:36
  400.0 12.6 %all_to_all.309 = f32[16,1,3072]{2,1,0:T(1,128)S(1)} all-to-all(f32[16,1,3072]{2,1,0:T(1,128)S(1)} %reshape.270), channel_id=1, replica_groups=mesh['row'=16,'col'=16] {'row'}, dimensions={0} | all-to-all | bytes 393216 | tf_op jit(solution)/shard_map/all_to_all | solution.py:71
  435.7 11.4 %all_to_all.310 = f32[16,1,3072]{2,1,0:T(1,128)S(1)} all-to-all(f32[16,1,3072]{2,1,0:T(1,128)S(1)} %reshape.272), channel_id=1, replica_groups=mesh['row'=16,'col'=16] {'col'}, dimensions={0} | all-to-all | bytes 393216 | tf_op jit(solution)/shard_map/all_to_all | solution.py:78
  457.0 12.2 %all_to_all.311 = f32[3,128,128]{2,0,1:T(4,128)S(1)} all-to-all(f32[3,128,128]{2,0,1:T(4,128)S(1)} %copy.413), channel_id=1, replica_groups=mesh['row'=16,'col'=16] {'col'}, dimensions={1} | all-to-all | bytes 393216 | tf_op jit(solution)/shard_map/all_to_all | solution.py:86
  472.5 13.6 %all_to_all.312 = f32[3,128,128]{2,0,1:T(4,128)S(1)} all-to-all(f32[3,128,128]{2,0,1:T(4,128)S(1)} %copy.418), channel_id=1, replica_groups=mesh['row'=16,'col'=16] {'row'}, dimensions={1} | all-to-all | bytes 393216 | tf_op jit(solution)/shard_map/all_to_all | solution.py:93
  512.3 18.5 %all_to_all.313 = f32[256,1,1]{2,1,0:T(1,128)S(1)} all-to-all(f32[256,1,1]{2,1,0:T(1,128)S(1)} %broadcast_in_dim.27), channel_id=1, replica_groups=mesh['row'=16,'col'=16] {'row','col'}, dimensions={0} | all-to-all | bytes 2048 | tf_op jit(solution)/shard_map/all_to_all | solution.py:36
  532.2 9.1 %all-to-all-start.16 = ((f32[256,1,1]{2,1,0:T(1,128)}), f32[256,1,1]{2,1,0:T(1,128)S(1)}, u32[]{:S(2)}, u32[]{:S(2)}) async-start(f32[256,1,1]{2,1,0:T(1,128)} %broadcast_in_dim.26), calls=%async_computation.16 | async-start | bytes 262144 | tf_op jit(solution)/shard_map/all_to_all | solution.py:36
  542.2 8.9 %all-to-all-done.16 = f32[256,1,1]{2,1,0:T(1,128)S(1)} async-done(((f32[256,1,1]{2,1,0:T(1,128)}), f32[256,1,1]{2,1,0:T(1,128)S(1)}, u32[]{:S(2)}, u32[]{:S(2)}) %all-to-all-start.16) | async-done | bytes 1056 | tf_op jit(solution)/shard_map/all_to_all | solution.py:36
  563.6 12.5 %all_to_all.314 = f32[16,1,3072]{2,1,0:T(1,128)S(1)} all-to-all(f32[16,1,3072]{2,1,0:T(1,128)S(1)} %reshape.274), channel_id=1, replica_groups=mesh['row'=16,'col'=16] {'row'}, dimensions={0} | all-to-all | bytes 393216 | tf_op jit(solution)/shard_map/all_to_all | solution.py:71
  588.1 5.9 fusion.17
  602.9 11.3 %all_to_all.315 = f32[16,1,3072]{2,1,0:T(1,128)S(1)} all-to-all(f32[16,1,3072]{2,1,0:T(1,128)S(1)} %reshape.276), channel_id=1, replica_groups=mesh['row'=16,'col'=16] {'col'}, dimensions={0} | all-to-all | bytes 393216 | tf_op jit(solution)/shard_map/all_to_all | solution.py:78
  624.1 11.9 %all_to_all.316 = f32[3,128,128]{2,0,1:T(4,128)S(1)} all-to-all(f32[3,128,128]{2,0,1:T(4,128)S(1)} %copy.434), channel_id=1, replica_groups=mesh['row'=16,'col'=16] {'col'}, dimensions={1} | all-to-all | bytes 393216 | tf_op jit(solution)/shard_map/all_to_all | solution.py:86
  639.4 13.6 %all_to_all.317 = f32[3,128,128]{2,0,1:T(4,128)S(1)} all-to-all(f32[3,128,128]{2,0,1:T(4,128)S(1)} %copy.439), channel_id=1, replica_groups=mesh['row'=16,'col'=16] {'row'}, dimensions={1} | all-to-all | bytes 393216 | tf_op jit(solution)/shard_map/all_to_all | solution.py:93
  656.4 7.9 %multiply_reduce_fusion = (f32[]{:T(128)}, f32[3,8,8,256]{3,2,1,0:T(8,128)}) fusion(f32[3,8,8,256]{3,2,1,0:T(8,128)} %copy-done.19, f32[1,8,8,256]{3,2,1,0:T(8,128)S(1)} %copy-done.22, f32[1,8,8,256]{3,2,1,0:T(8,128)} %copy-done.25, f32[1,8,8,256]{3,2,1,0:T(8,128)} %copy-done.24, f32[]{:T(128)S(6)} %div.37, f32[3,8,256,8]{3,2,1,0:T(8,128)S(1)} %reshape.257), kind=kOutput, calls=%fused_computation.88 | convolution fusion | flops 152272896 | bytes 786440 | tf_op jit(solution)/shard_map/kx,cyxz->cyzk/dot_general | solution.py:94
  665.0 18.9 %all_to_all.318 = f32[256,1,1]{2,1,0:T(1,128)S(1)} all-to-all(f32[256,1,1]{2,1,0:T(1,128)S(1)} %broadcast_in_dim.28), channel_id=1, replica_groups=mesh['row'=16,'col'=16] {'row','col'}, dimensions={0} | all-to-all | bytes 2048 | tf_op jit(solution)/shard_map/all_to_all | solution.py:36
  705.2 17.9 %all_to_all.319 = f32[256,1,1]{2,1,0:T(1,128)S(1)} all-to-all(f32[256,1,1]{2,1,0:T(1,128)S(1)} %broadcast_in_dim.29), channel_id=1, replica_groups=mesh['row'=16,'col'=16] {'row','col'}, dimensions={0} | all-to-all | bytes 2048 | tf_op jit(solution)/shard_map/all_to_all | solution.py:36
  (441 shorter events, 355.2 us)
Async XLA Ops:
  1.5 7.0 collective-permute-start
  1.6 7.0 collective-permute-start.1
  9.8 4.2 collective-permute-start.2
  10.0 7.5 %collective-permute-start.3 = (f32[5,10,1,256]{3,2,1,0:T(1,128)S(1)}, f32[5,10,1,256]{3,2,1,0:T(1,128)S(1)}, u32[]{:S(2)}, u32[]{:S(2)}) collective-permute-start(f32[5,10,1,256]{3,2,1,0:T(1,128)S(1)} %get-tuple-element.50), channel_id=1, source_target_pairs={{1,0},{2,1},{3,2},{4,3},{5,4},{6,5},{7,6},{8,7},{9,8},{10,9},{11,1... | collective-permute-start | bytes 153608 | tf_op jit(solution)/shard_map/ppermute | solution.py:26
  31.7 16.3 %all-to-all-start = ((f32[16,1,3072]{2,1,0:T(1,128)}), f32[16,1,3072]{2,1,0:T(1,128)S(1)}, u32[]{:S(2)}, u32[]{:S(2)}) async-start(f32[16,1,3072]{2,1,0:T(1,128)} %reshape.262), calls=%async_computation | async-start | bytes 393216 | tf_op jit(solution)/shard_map/all_to_all | solution.py:71
  76.0 11.5 %all-to-all-start.1 = ((f32[16,1,3072]{2,1,0:T(1,128)}), f32[16,1,3072]{2,1,0:T(1,128)S(1)}, u32[]{:S(2)}, u32[]{:S(2)}) async-start(f32[16,1,3072]{2,1,0:T(1,128)} %reshape.264), calls=%async_computation.1 | async-start | bytes 393216 | tf_op jit(solution)/shard_map/all_to_all | solution.py:78
  135.6 4.5 collective-permute-start.4
  140.1 5.7 collective-permute-start.6
  144.3 7.2 collective-permute-start.7
  174.1 18.9 %all-to-all-start.4 = ((f32[256,1,1]{2,1,0:T(1,128)}), f32[256,1,1]{2,1,0:T(1,128)S(1)}, u32[]{:S(2)}, u32[]{:S(2)}) async-start(f32[256,1,1]{2,1,0:T(1,128)} %broadcast_in_dim.22), calls=%async_computation.4 | async-start | bytes 262144 | tf_op jit(solution)/shard_map/all_to_all | solution.py:36
  329.5 4.5 collective-permute-start.8
  329.5 4.5 collective-permute-start.9
  334.1 5.3 collective-permute-start.10
  337.8 7.2 collective-permute-start.11
  367.8 4.5 collective-permute-start.12
  367.9 4.5 collective-permute-start.13
  372.4 5.3 collective-permute-start.14
  376.1 7.2 collective-permute-start.15
  384.5 4.3 collective-permute-start.16
  384.5 4.3 collective-permute-start.17
  493.5 4.5 collective-permute-start.18
  498.0 5.7 collective-permute-start.20
  502.1 7.2 collective-permute-start.21
  532.2 18.9 %all-to-all-start.16 = ((f32[256,1,1]{2,1,0:T(1,128)}), f32[256,1,1]{2,1,0:T(1,128)S(1)}, u32[]{:S(2)}, u32[]{:S(2)}) async-start(f32[256,1,1]{2,1,0:T(1,128)} %broadcast_in_dim.26), calls=%async_computation.16 | async-start | bytes 262144 | tf_op jit(solution)/shard_map/all_to_all | solution.py:36
  687.1 4.5 collective-permute-start.22
  687.1 4.5 collective-permute-start.23
  691.6 5.3 collective-permute-start.24
  695.4 7.2 collective-permute-start.25
  725.4 4.5 collective-permute-start.26
  725.4 4.5 collective-permute-start.27
  729.9 5.3 collective-permute-start.28
  733.7 7.2 collective-permute-start.29
  (56 other events, 795.3 us)
where the time goes:
time: 750 us; the launch traced here: 742 us
  blocking collectives  285 us (38%)
  local copies, waits for them, and re-layouts  171 us (23%)
  waiting for transfers between devices  92.7 us (12%)
  starting transfers between devices  80.1 us (11%)
  matrix products  71.2 us (9%)
  other arithmetic  31.2 us (4%)
  between operations  11 us (1%)
    all_to_all x6, blocking collectives, global_sum(): gathered = lax.all_to_all(spread, ('row', 'col'), 0, 0, tiled=True)  110 us
    unnamed x124, local copies, waits for them, and re-layouts  70.6 us
    all_to_all x4, blocking collectives, precondition(): lax.all_to_all(spectrum, 'row', split_axis=1, concat_axis=2, tiled=True)  54.6 us
    all_to_all x4, blocking collectives, precondition(): lax.all_to_all(spectrum, 'col', split_axis=1, concat_axis=2, tiled=True)  48.3 us
    all_to_all x3, blocking collectives, precondition(): lax.all_to_all(spectrum, 'row', split_axis=2, concat_axis=1, tiled=True)  37.7 us
    ppermute x14, waiting for transfers between devices, padded(): lax.ppermute(head, axis, [((i + 1) % count, i) for i in range(count)])  36.5 us
    all_to_all x3, blocking collectives, precondition(): lax.all_to_all(spectrum, 'col', split_axis=2, concat_axis=1, tiled=True)  34 us
    dot_general x4, matrix products, precondition(): jnp.einsum('kx,cyxz->cyzk', xtable, spectrum.reshape(components, owned_he...  27.1 us
  transfers between devices with their start and end apart: 34, of which 26 were waited for; matrix products, arithmetic and copies ran while one was open for 1% of the time, Pallas kernels for 0%

commit v1 on v0

--- a/solution.py
+++ b/solution.py
@@ -12,6 +12,12 @@
 ANCHOR = 0.002
 RAYLEIGH_NUMBER = 1.0
 SMOOTHING = 2.0
+
+
+def swap_blocks(shard, axis, split, join):
+    pieces = jnp.split(shard, lax.axis_size(axis), axis=split)
+    arrived = lax.all_to_all(jnp.stack(pieces), axis, 0, 0)
+    return jnp.concatenate(arrived, axis=join)
 
 
 def padded(cells, sides, width):
@@ -68,7 +74,7 @@
     spectrum = jnp.einsum("kx,cyzx->cykz", xtable, residual, precision=PRECISE).reshape(
         components, owned_height_lines, period_extent_first * owned_depth_slices
     )
-    spectrum = lax.all_to_all(spectrum, "row", split_axis=2, concat_axis=1, tiled=True)
+    spectrum = swap_blocks(spectrum, "row", 2, 1)
     spectrum = jnp.einsum(
         "ky,cyxz->czkx",
         ytable,

time: 750 us -> 733 us (0.977)
  matrix products: 71.2 us -> 55.7 us
    another operation x0 -> x12, local copies, waits for them, and re-layouts: none -> 18 us  [the longest x8 15.2 us: precondition(): spectrum.reshape(components, ylength, xpiece, owned_depth_slices)]
    dot_general x4, matrix products: 22.9 us -> 5.1 us  [precondition(): jnp.einsum('ky,cyxz->czkx', ytable, spectrum.reshape(components, ylength,...]
    all_to_all x5 -> x0, local copies, waits for them, and re-layouts: 16.5 us -> none  [precondition(): lax.all_to_all(spectrum, 'row', split_axis=2, concat_axis=1, tiled=True)]
    reshape x4 -> x0, local copies, waits for them, and re-layouts: 9.64 us -> none  [precondition(): spectrum.reshape(components, ylength, xpiece, owned_depth_slices)]
    unnamed x124 -> x178, local copies, waits for them, and re-layouts: 70.6 us -> 79.1 us
where the time goes in v1:
time: 733 us; the launch traced here: 721 us
  blocking collectives  286 us (39%)
  local copies, waits for them, and re-layouts  168 us (23%)
  waiting for transfers between devices  91.8 us (13%)
  starting transfers between devices  80.7 us (11%)
  matrix products  55.7 us (8%)
  other arithmetic  28.5 us (4%)
  between operations  10.9 us (1%)
    all_to_all x6, blocking collectives, global_sum(): gathered = lax.all_to_all(spread, ('row', 'col'), 0, 0, tiled=True)  111 us
    unnamed x178, local copies, waits for them, and re-layouts  79.1 us
    all_to_all x4, blocking collectives, precondition(): lax.all_to_all(spectrum, 'row', split_axis=1, concat_axis=2, tiled=True)  54.6 us
    all_to_all x4, blocking collectives, precondition(): lax.all_to_all(spectrum, 'col', split_axis=1, concat_axis=2, tiled=True)  47.1 us
    all_to_all x3, blocking collectives, swap_blocks(): arrived = lax.all_to_all(jnp.stack(pieces), axis, 0, 0)  38.6 us
    ppermute x14, waiting for transfers between devices, padded(): lax.ppermute(head, axis, [((i + 1) % count, i) for i in range(count)])  37.1 us
    all_to_all x3, blocking collectives, precondition(): lax.all_to_all(spectrum, 'col', split_axis=2, concat_axis=1, tiled=True)  34.4 us
    dot_general x4, matrix products, precondition(): jnp.einsum('kx,cyxz->cyzk', xtable, spectrum.reshape(components, owned_he...  27.1 us
  transfers between devices with their start and end apart: 34, of which 26 were waited for; matrix products, arithmetic and copies ran while one was open for 1% of the time, Pallas kernels for 0%

profile of v1, /device:TPU:30, one launch (start us, length us, event | category | flops | bytes accessed | tf_op | source)
XLA Modules:
  0.0 721.2 jit_solution(16085163063137593767)
XLA Ops:
  50.4 6.2 all-to-all-start
  58.6 8.0 %all-to-all-done = f32[16,3,8,128]{3,2,1,0:T(8,128)S(1)} async-done(((f32[16,3,8,128]{3,2,1,0:T(8,128)}), f32[16,3,8,128]{3,2,1,0:T(8,128)S(1)}, u32[]{:S(2)}, u32[]{:S(2)}) %all-to-all-start) | async-done | bytes 196640 | tf_op jit(solution)/shard_map/all_to_all | solution.py:19
  81.3 7.2 %all-to-all-start.1 = ((f32[16,1,3072]{2,1,0:T(1,128)}), f32[16,1,3072]{2,1,0:T(1,128)S(1)}, u32[]{:S(2)}, u32[]{:S(2)}) async-start(f32[16,1,3072]{2,1,0:T(1,128)} %reshape.262), calls=%async_computation.1 | async-start | bytes 393216 | tf_op jit(solution)/shard_map/all_to_all | solution.py:84
  103.7 11.7 %all_to_all.260 = f32[3,128,128]{2,0,1:T(4,128)S(1)} all-to-all(f32[3,128,128]{2,0,1:T(4,128)S(1)} %copy.405), channel_id=1, replica_groups=mesh['row'=16,'col'=16] {'col'}, dimensions={1} | all-to-all | bytes 393216 | tf_op jit(solution)/shard_map/all_to_all | solution.py:92
  118.8 13.7 %all_to_all.261 = f32[3,128,128]{2,0,1:T(4,128)S(1)} all-to-all(f32[3,128,128]{2,0,1:T(4,128)S(1)} %copy.410), channel_id=1, replica_groups=mesh['row'=16,'col'=16] {'row'}, dimensions={1} | all-to-all | bytes 393216 | tf_op jit(solution)/shard_map/all_to_all | solution.py:99
  151.7 5.8 collective-permute-done.7
  160.5 18.4 %all_to_all.262 = f32[256,1,1]{2,1,0:T(1,128)S(1)} all-to-all(f32[256,1,1]{2,1,0:T(1,128)S(1)} %broadcast_in_dim.23), channel_id=1, replica_groups=mesh['row'=16,'col'=16] {'row','col'}, dimensions={0} | all-to-all | bytes 2048 | tf_op jit(solution)/shard_map/all_to_all | solution.py:42
  180.3 8.9 %all-to-all-start.4 = ((f32[256,1,1]{2,1,0:T(1,128)}), f32[256,1,1]{2,1,0:T(1,128)S(1)}, u32[]{:S(2)}, u32[]{:S(2)}) async-start(f32[256,1,1]{2,1,0:T(1,128)} %broadcast_in_dim.22), calls=%async_computation.4 | async-start | bytes 262144 | tf_op jit(solution)/shard_map/all_to_all | solution.py:42
  190.1 8.8 %all-to-all-done.4 = f32[256,1,1]{2,1,0:T(1,128)S(1)} async-done(((f32[256,1,1]{2,1,0:T(1,128)}), f32[256,1,1]{2,1,0:T(1,128)S(1)}, u32[]{:S(2)}, u32[]{:S(2)}) %all-to-all-start.4) | async-done | bytes 1056 | tf_op jit(solution)/shard_map/all_to_all | solution.py:42
  219.3 13.1 %all_to_all.263 = f32[16,3,8,128]{3,2,1,0:T(8,128)} all-to-all(f32[16,3,8,128]{3,2,1,0:T(8,128)S(1)} %constant_dynamic-update-slice_fusion.16), channel_id=1, replica_groups=mesh['row'=16,'col'=16] {'row'}, dimensions={0} | all-to-all | bytes 393216 | tf_op jit(solution)/shard_map/all_to_all | solution.py:19
  245.9 11.5 %all_to_all.264 = f32[16,1,3072]{2,1,0:T(1,128)S(1)} all-to-all(f32[16,1,3072]{2,1,0:T(1,128)S(1)} %reshape.264), channel_id=1, replica_groups=mesh['row'=16,'col'=16] {'col'}, dimensions={0} | all-to-all | bytes 393216 | tf_op jit(solution)/shard_map/all_to_all | solution.py:84
  267.3 11.8 %all_to_all.265 = f32[3,128,128]{2,0,1:T(4,128)S(1)} all-to-all(f32[3,128,128]{2,0,1:T(4,128)S(1)} %copy.424), channel_id=1, replica_groups=mesh['row'=16,'col'=16] {'col'}, dimensions={1} | all-to-all | bytes 393216 | tf_op jit(solution)/shard_map/all_to_all | solution.py:92
  282.4 13.6 %all_to_all.266 = f32[3,128,128]{2,0,1:T(4,128)S(1)} all-to-all(f32[3,128,128]{2,0,1:T(4,128)S(1)} %copy.429), channel_id=1, replica_groups=mesh['row'=16,'col'=16] {'row'}, dimensions={1} | all-to-all | bytes 393216 | tf_op jit(solution)/shard_map/all_to_all | solution.py:99
  299.5 8.0 %multiply_reduce_fusion.3 = (f32[]{:T(128)}, f32[3,8,8,256]{3,2,1,0:T(8,128)}) fusion(f32[3,8,8,256]{3,2,1,0:T(8,128)} %copy-done.17, f32[1,8,8,256]{3,2,1,0:T(8,128)} %copy-done.24, f32[1,8,8,256]{3,2,1,0:T(8,128)} %copy-done.28, f32[1,8,8,256]{3,2,1,0:T(8,128)} %copy-done.27, f32[]{:T(128)S(6)} %div.34, f32[3,8,256,8]{3,2,1,0:T(8,128)S(1)} %reshape.241), kind=kOutput, calls=%fused_computation.86 | convolution fusion | flops 152272896 | bytes 786440 | tf_op jit(solution)/shard_map/kx,cyxz->cyzk/dot_general | solution.py:100
  308.2 19.2 %all_to_all.267 = f32[256,1,1]{2,1,0:T(1,128)S(1)} all-to-all(f32[256,1,1]{2,1,0:T(1,128)S(1)} %broadcast_in_dim.24), channel_id=1, replica_groups=mesh['row'=16,'col'=16] {'row','col'}, dimensions={0} | all-to-all | bytes 2048 | tf_op jit(solution)/shard_map/all_to_all | solution.py:42
  340.6 5.6 collective-permute-done.11
  348.9 17.9 %all_to_all.268 = f32[256,1,1]{2,1,0:T(1,128)S(1)} all-to-all(f32[256,1,1]{2,1,0:T(1,128)S(1)} %broadcast_in_dim.25), channel_id=1, replica_groups=mesh['row'=16,'col'=16] {'row','col'}, dimensions={0} | all-to-all | bytes 2048 | tf_op jit(solution)/shard_map/all_to_all | solution.py:42
  379.0 5.6 collective-permute-done.15
  396.2 12.5 %all_to_all.269 = f32[16,3,8,128]{3,2,1,0:T(8,128)S(1)} all-to-all(f32[16,3,8,128]{3,2,1,0:T(8,128)S(1)} %constant_dynamic-update-slice_fusion.32), channel_id=1, replica_groups=mesh['row'=16,'col'=16] {'row'}, dimensions={0} | all-to-all | bytes 393216 | tf_op jit(solution)/shard_map/all_to_all | solution.py:19
  419.8 11.2 %all_to_all.270 = f32[16,1,3072]{2,1,0:T(1,128)S(1)} all-to-all(f32[16,1,3072]{2,1,0:T(1,128)S(1)} %reshape.266), channel_id=1, replica_groups=mesh['row'=16,'col'=16] {'col'}, dimensions={0} | all-to-all | bytes 393216 | tf_op jit(solution)/shard_map/all_to_all | solution.py:84
  440.9 12.0 %all_to_all.271 = f32[3,128,128]{2,0,1:T(4,128)S(1)} all-to-all(f32[3,128,128]{2,0,1:T(4,128)S(1)} %copy.443), channel_id=1, replica_groups=mesh['row'=16,'col'=16] {'col'}, dimensions={1} | all-to-all | bytes 393216 | tf_op jit(solution)/shard_map/all_to_all | solution.py:92
  456.2 13.7 %all_to_all.272 = f32[3,128,128]{2,0,1:T(4,128)S(1)} all-to-all(f32[3,128,128]{2,0,1:T(4,128)S(1)} %copy.448), channel_id=1, replica_groups=mesh['row'=16,'col'=16] {'row'}, dimensions={1} | all-to-all | bytes 393216 | tf_op jit(solution)/shard_map/all_to_all | solution.py:99
  496.1 18.4 %all_to_all.273 = f32[256,1,1]{2,1,0:T(1,128)S(1)} all-to-all(f32[256,1,1]{2,1,0:T(1,128)S(1)} %broadcast_in_dim.27), channel_id=1, replica_groups=mesh['row'=16,'col'=16] {'row','col'}, dimensions={0} | all-to-all | bytes 2048 | tf_op jit(solution)/shard_map/all_to_all | solution.py:42
  515.8 9.3 %all-to-all-start.16 = ((f32[256,1,1]{2,1,0:T(1,128)}), f32[256,1,1]{2,1,0:T(1,128)S(1)}, u32[]{:S(2)}, u32[]{:S(2)}) async-start(f32[256,1,1]{2,1,0:T(1,128)} %broadcast_in_dim.26), calls=%async_computation.16 | async-start | bytes 262144 | tf_op jit(solution)/shard_map/all_to_all | solution.py:42
  526.0 8.9 %all-to-all-done.16 = f32[256,1,1]{2,1,0:T(1,128)S(1)} async-done(((f32[256,1,1]{2,1,0:T(1,128)}), f32[256,1,1]{2,1,0:T(1,128)S(1)}, u32[]{:S(2)}, u32[]{:S(2)}) %all-to-all-start.16) | async-done | bytes 1056 | tf_op jit(solution)/shard_map/all_to_all | solution.py:42
  555.1 13.1 %all_to_all.274 = f32[16,3,8,128]{3,2,1,0:T(8,128)} all-to-all(f32[16,3,8,128]{3,2,1,0:T(8,128)S(1)} %constant_dynamic-update-slice_fusion.48), channel_id=1, replica_groups=mesh['row'=16,'col'=16] {'row'}, dimensions={0} | all-to-all | bytes 393216 | tf_op jit(solution)/shard_map/all_to_all | solution.py:19
  581.7 11.6 %all_to_all.275 = f32[16,1,3072]{2,1,0:T(1,128)S(1)} all-to-all(f32[16,1,3072]{2,1,0:T(1,128)S(1)} %reshape.268), channel_id=1, replica_groups=mesh['row'=16,'col'=16] {'col'}, dimensions={0} | all-to-all | bytes 393216 | tf_op jit(solution)/shard_map/all_to_all | solution.py:84
  603.2 11.7 %all_to_all.276 = f32[3,128,128]{2,0,1:T(4,128)S(1)} all-to-all(f32[3,128,128]{2,0,1:T(4,128)S(1)} %copy.462), channel_id=1, replica_groups=mesh['row'=16,'col'=16] {'col'}, dimensions={1} | all-to-all | bytes 393216 | tf_op jit(solution)/shard_map/all_to_all | solution.py:92
  618.2 13.6 %all_to_all.277 = f32[3,128,128]{2,0,1:T(4,128)S(1)} all-to-all(f32[3,128,128]{2,0,1:T(4,128)S(1)} %copy.467), channel_id=1, replica_groups=mesh['row'=16,'col'=16] {'row'}, dimensions={1} | all-to-all | bytes 393216 | tf_op jit(solution)/shard_map/all_to_all | solution.py:99
  635.2 7.9 %multiply_reduce_fusion = (f32[]{:T(128)}, f32[3,8,8,256]{3,2,1,0:T(8,128)}) fusion(f32[3,8,8,256]{3,2,1,0:T(8,128)} %copy-done.19, f32[1,8,8,256]{3,2,1,0:T(8,128)S(1)} %copy-done.23, f32[1,8,8,256]{3,2,1,0:T(8,128)} %copy-done.26, f32[1,8,8,256]{3,2,1,0:T(8,128)} %copy-done.25, f32[]{:T(128)S(6)} %div.37, f32[3,8,256,8]{3,2,1,0:T(8,128)S(1)} %reshape.253), kind=kOutput, calls=%fused_computation.80 | convolution fusion | flops 152272896 | bytes 786440 | tf_op jit(solution)/shard_map/kx,cyxz->cyzk/dot_general | solution.py:100
  643.8 19.0 %all_to_all.278 = f32[256,1,1]{2,1,0:T(1,128)S(1)} all-to-all(f32[256,1,1]{2,1,0:T(1,128)S(1)} %broadcast_in_dim.28), channel_id=1, replica_groups=mesh['row'=16,'col'=16] {'row','col'}, dimensions={0} | all-to-all | bytes 2048 | tf_op jit(solution)/shard_map/all_to_all | solution.py:42
  684.2 17.9 %all_to_all.279 = f32[256,1,1]{2,1,0:T(1,128)S(1)} all-to-all(f32[256,1,1]{2,1,0:T(1,128)S(1)} %broadcast_in_dim.29), channel_id=1, replica_groups=mesh['row'=16,'col'=16] {'row','col'}, dimensions={0} | all-to-all | bytes 2048 | tf_op jit(solution)/shard_map/all_to_all | solution.py:42
  (499 shorter events, 334.4 us)
Async XLA Ops:
  1.5 7.0 collective-permute-start
  1.6 7.0 collective-permute-start.1
  9.8 4.2 collective-permute-start.2
  10.6 7.4 %collective-permute-start.3 = (f32[5,10,1,256]{3,2,1,0:T(1,128)S(1)}, f32[5,10,1,256]{3,2,1,0:T(1,128)S(1)}, u32[]{:S(2)}, u32[]{:S(2)}) collective-permute-start(f32[5,10,1,256]{3,2,1,0:T(1,128)S(1)} %get-tuple-element.50), channel_id=1, source_target_pairs={{1,0},{2,1},{3,2},{4,3},{5,4},{6,5},{7,6},{8,7},{9,8},{10,9},{11,1... | collective-permute-start | bytes 153608 | tf_op jit(solution)/shard_map/ppermute | solution.py:32
  50.4 16.1 %all-to-all-start = ((f32[16,3,8,128]{3,2,1,0:T(8,128)}), f32[16,3,8,128]{3,2,1,0:T(8,128)S(1)}, u32[]{:S(2)}, u32[]{:S(2)}) async-start(f32[16,3,8,128]{3,2,1,0:T(8,128)} %constant_dynamic-update-slice_fusion), calls=%async_computation | async-start | bytes 393216 | tf_op jit(solution)/shard_map/all_to_all | solution.py:19
  81.3 12.0 %all-to-all-start.1 = ((f32[16,1,3072]{2,1,0:T(1,128)}), f32[16,1,3072]{2,1,0:T(1,128)S(1)}, u32[]{:S(2)}, u32[]{:S(2)}) async-start(f32[16,1,3072]{2,1,0:T(1,128)} %reshape.262), calls=%async_computation.1 | async-start | bytes 393216 | tf_op jit(solution)/shard_map/all_to_all | solution.py:84
  141.5 4.5 collective-permute-start.4
  146.0 5.7 collective-permute-start.6
  150.1 7.4 %collective-permute-start.7 = (f32[3,10,1,256]{3,2,1,0:T(1,128)S(1)}, f32[3,10,1,256]{3,2,1,0:T(1,128)S(1)}, u32[]{:S(2)}, u32[]{:S(2)}) collective-permute-start(f32[3,10,1,256]{3,2,1,0:T(1,128)S(1)} %get-tuple-element.95), channel_id=1, source_target_pairs={{1,0},{2,1},{3,2},{4,3},{5,4},{6,5},{7,6},{8,7},{9,8},{10,9},{11,1... | collective-permute-start | bytes 92168 | tf_op jit(solution)/shard_map/ppermute | solution.py:32
  180.3 18.7 %all-to-all-start.4 = ((f32[256,1,1]{2,1,0:T(1,128)}), f32[256,1,1]{2,1,0:T(1,128)S(1)}, u32[]{:S(2)}, u32[]{:S(2)}) async-start(f32[256,1,1]{2,1,0:T(1,128)} %broadcast_in_dim.22), calls=%async_computation.4 | async-start | bytes 262144 | tf_op jit(solution)/shard_map/all_to_all | solution.py:42
  330.7 4.5 collective-permute-start.8
  330.7 4.5 collective-permute-start.9
  335.2 5.4 collective-permute-start.10
  339.0 7.2 %collective-permute-start.11 = (f32[3,10,1,256]{3,2,1,0:T(1,128)S(1)}, f32[3,10,1,256]{3,2,1,0:T(1,128)S(1)}, u32[]{:S(2)}, u32[]{:S(2)}) collective-permute-start(f32[3,10,1,256]{3,2,1,0:T(1,128)S(1)} %get-tuple-element.93), channel_id=1, source_target_pairs={{1,0},{2,1},{3,2},{4,3},{5,4},{6,5},{7,6},{8,7},{9,8},{10,9},{11,1... | collective-permute-start | bytes 92168 | tf_op jit(solution)/shard_map/ppermute | solution.py:32
  369.1 4.5 collective-permute-start.12
  369.1 4.5 collective-permute-start.13
  373.6 5.3 collective-permute-start.14
  377.4 7.2 %collective-permute-start.15 = (f32[3,10,1,256]{3,2,1,0:T(1,128)S(1)}, f32[3,10,1,256]{3,2,1,0:T(1,128)S(1)}, u32[]{:S(2)}, u32[]{:S(2)}) collective-permute-start(f32[3,10,1,256]{3,2,1,0:T(1,128)S(1)} %get-tuple-element.91), channel_id=1, source_target_pairs={{1,0},{2,1},{3,2},{4,3},{5,4},{6,5},{7,6},{8,7},{9,8},{10,9},{11,1... | collective-permute-start | bytes 92168 | tf_op jit(solution)/shard_map/ppermute | solution.py:32
  385.7 4.3 collective-permute-start.16
  385.7 4.3 collective-permute-start.17
  477.3 4.5 collective-permute-start.18
  481.9 5.7 collective-permute-start.20
  486.0 7.2 %collective-permute-start.21 = (f32[3,10,1,256]{3,2,1,0:T(1,128)S(1)}, f32[3,10,1,256]{3,2,1,0:T(1,128)S(1)}, u32[]{:S(2)}, u32[]{:S(2)}) collective-permute-start(f32[3,10,1,256]{3,2,1,0:T(1,128)S(1)} %get-tuple-element.89), channel_id=1, source_target_pairs={{1,0},{2,1},{3,2},{4,3},{5,4},{6,5},{7,6},{8,7},{9,8},{10,9},{11,1... | collective-permute-start | bytes 92168 | tf_op jit(solution)/shard_map/ppermute | solution.py:32
  515.8 19.1 %all-to-all-start.16 = ((f32[256,1,1]{2,1,0:T(1,128)}), f32[256,1,1]{2,1,0:T(1,128)S(1)}, u32[]{:S(2)}, u32[]{:S(2)}) async-start(f32[256,1,1]{2,1,0:T(1,128)} %broadcast_in_dim.26), calls=%async_computation.16 | async-start | bytes 262144 | tf_op jit(solution)/shard_map/all_to_all | solution.py:42
  666.1 4.5 collective-permute-start.22
  666.1 4.5 collective-permute-start.23
  670.6 5.4 collective-permute-start.24
  674.4 7.2 %collective-permute-start.25 = (f32[3,10,1,256]{3,2,1,0:T(1,128)S(1)}, f32[3,10,1,256]{3,2,1,0:T(1,128)S(1)}, u32[]{:S(2)}, u32[]{:S(2)}) collective-permute-start(f32[3,10,1,256]{3,2,1,0:T(1,128)S(1)} %get-tuple-element.87), channel_id=1, source_target_pairs={{1,0},{2,1},{3,2},{4,3},{5,4},{6,5},{7,6},{8,7},{9,8},{10,9},{11,1... | collective-permute-start | bytes 92168 | tf_op jit(solution)/shard_map/ppermute | solution.py:32
  704.4 4.5 collective-permute-start.26
  704.4 4.5 collective-permute-start.27
  708.9 5.3 collective-permute-start.28
  712.7 7.2 %collective-permute-start.29 = (f32[3,10,1,256]{3,2,1,0:T(1,128)S(1)}, f32[3,10,1,256]{3,2,1,0:T(1,128)S(1)}, u32[]{:S(2)}, u32[]{:S(2)}) collective-permute-start(f32[3,10,1,256]{3,2,1,0:T(1,128)S(1)} %get-tuple-element.85), channel_id=1, source_target_pairs={{1,0},{2,1},{3,2},{4,3},{5,4},{6,5},{7,6},{8,7},{9,8},{10,9},{11,1... | collective-permute-start | bytes 92168 | tf_op jit(solution)/shard_map/ppermute | solution.py:32
  (57 other events, 657.2 us)
